TPU v7x, 256 devices: a whole 4x4x8 slice. The times are simulated.
256 devices in a mesh: gx: 32 (over y, z_hi, core), gz: 8 (over z_lo, x).
Axes of the slice: x: 4, y: 4, z: 8 (z_hi: 4, z_lo: 2; z = z_hi * 2 + z_lo), core: 2. Of those that a mesh axis runs over, the one named last changes fastest.
Arguments:
- scalars: float32 [2, 4096, 128, 256], P(None, 'gx', 'gz'), may hold values from -6 to 6
- diffusivity: float32 [4096, 128, 256], P('gx', 'gz'), may hold values from 0.01 to 0.1
- reaction_rate: float32 [4096, 128, 256], P('gx', 'gz'), may hold values from 0.05 to 1
- block_inverse: float32 [2, 32, 128, 128], P(None, 'gx'), may hold values from 0 to 1
- block_response: float32 [2, 32, 128], P(None, 'gx'), may hold values from 0 to 1, as said below
- mean_profile: float32 [2, 256], replicated, may hold values from -4 to 4
- recycle_gain: float32 [2, 256], replicated, may hold values from 0.5 to 1.5
- station_index: int32 [1], replicated, may hold values from 0 to 4095
- span_shift: int32 [1], replicated, may hold values from 0 to 127
Outputs:
- transported: float32 [2, 4096, 128, 256], P(None, 'gx', 'gz')
Inputs may be any that keep to these rules, and one draw needn't show every extreme that they name: `block_response`: every entry is positive.
All inputs are finite; a program needn't handle non-finite values.
Results may differ from a plain program's by a relative error of at most 0.0003.
Values sent between devices are 32-bit elements; how exact they have to be, the bound alone decides.
No kernel may reach another device: no remote copies, remote signals or barrier semaphores. Data moves between devices by JAX's collectives and lax.ppermute only.
A program may use at most 64 MiB of HBM per device.

v0:
```python
import jax
import jax.numpy as jnp
from jax import lax
from jax.sharding import PartitionSpec as P

reaction_yields = (-1.0, 1.0)


def from_root(x, axis, root):
    mine = lax.axis_index(axis) == root
    return lax.psum(jnp.where(mine, x, jnp.zeros_like(x)), axis)


def with_halo(x, sides, width, wrap):
    for axis, dim in sides:
        devices, length = (lax.axis_size(axis), x.shape[dim])
        up = [(i, (i + 1) % devices) for i in range(devices if wrap else devices - 1)]
        down = [(j, i) for i, j in up]
        last = lax.slice_in_dim(x, length - width, length, axis=dim)
        first = lax.slice_in_dim(x, 0, width, axis=dim)
        before = lax.ppermute(last, axis, up)
        after = lax.ppermute(first, axis, down)
        x = jnp.concatenate([before, x, after], axis=dim)
    return x


def prefix(part, axis, combine, identity):
    place = lax.axis_index(axis)
    gathered = jax.tree.map(lambda a: lax.all_gather(a, axis), part)
    state = jax.tree.map(lambda a, e: jnp.zeros_like(a) + jnp.asarray(e, a.dtype), part, identity)

    def one(hop, state):
        return combine(
            state, jax.tree.map(lambda a: lax.dynamic_index_in_dim(a, hop, 0, False), gathered)
        )

    return lax.fori_loop(0, place, one, state)


def fourth_order(padded, dimension, length):

    def shifted(offset):
        return lax.slice_in_dim(padded, offset, offset + length, axis=dimension)

    return (
        -shifted(0) + 16.0 * shifted(1) - 30.0 * shifted(2) + 16.0 * shifted(3) - shifted(4)
    ) / 12.0


def make_inflow(station_plane, mean_profile, recycle_gain, span_shift):
    span_mean = jnp.mean(station_plane, axis=1, keepdims=True)
    rolled = jnp.roll(station_plane, span_shift[0], axis=1)
    return mean_profile[:, None, :] + recycle_gain[:, None, :] * (rolled - span_mean)


def explicit_part(stream_padded, span_padded, center, diffusivity, reaction_rate):
    wall_padded = jnp.pad(center, ((0, 0), (0, 0), (0, 0), (2, 2)))
    laplacian = fourth_order(stream_padded, 1, center.shape[1])
    laplacian = laplacian + fourth_order(span_padded, 2, center.shape[2])
    laplacian = laplacian + fourth_order(wall_padded, 3, center.shape[3])
    reaction = reaction_rate * jax.nn.softplus(center[0]) * jax.nn.softplus(center[1])
    source = jnp.stack([reaction_yields[0] * reaction, reaction_yields[1] * reaction])
    return center + diffusivity[None] * laplacian + source


def on_device(
    scalars,
    diffusivity,
    reaction_rate,
    block_inverse,
    block_response,
    mean_profile,
    recycle_gain,
    station_index,
    span_shift,
):
    plane_count = scalars.shape[1]
    span_cells = scalars.shape[2]
    stream_devices = lax.axis_size("gx")
    stream_rank = lax.axis_index("gx")
    span_rank = lax.axis_index("gz")
    owner_row = station_index[0] // plane_count
    local_plane = station_index[0] - owner_row * plane_count
    own_slice = lax.dynamic_index_in_dim(scalars, local_plane, 1, keepdims=False)
    arrived = from_root(own_slice, "gx", owner_row)
    station_plane = lax.all_gather(arrived, "gz", axis=1, tiled=True)
    inflow_full = make_inflow(station_plane, mean_profile, recycle_gain, span_shift)
    inflow = lax.dynamic_slice_in_dim(inflow_full, span_rank * span_cells, span_cells, 1)
    stream_padded = with_halo(scalars, (("gx", 1),), 2, False)
    edge_shape = (scalars.shape[0], 2, scalars.shape[2], scalars.shape[3])
    inlet_planes = jnp.broadcast_to(inflow[:, None], edge_shape)
    outlet_planes = jnp.broadcast_to(scalars[:, -1:], edge_shape)
    head_planes = jnp.where(stream_rank == 0, inlet_planes, stream_padded[:, :2])
    tail_planes = jnp.where(stream_rank == stream_devices - 1, outlet_planes, stream_padded[:, -2:])
    window = jnp.concatenate([head_planes, stream_padded[:, 2:-2], tail_planes], axis=1)
    span_padded = with_halo(scalars, (("gz", 2),), 2, True)
    explicit = explicit_part(window, span_padded, scalars, diffusivity, reaction_rate)
    local_part = jnp.einsum(
        "sij,sjzy->sizy", block_inverse[:, 0], explicit, precision=lax.Precision.HIGHEST
    )
    response = block_response[:, 0]
    exit_plane = local_part[:, -1]
    exit_ratio = response[:, -1]

    def compose(earlier_part, later_part):
        return (
            earlier_part[0] * later_part[0],
            later_part[0][:, None, None] * earlier_part[1] + later_part[1],
        )

    identity = (jnp.ones_like(exit_ratio), jnp.zeros_like(exit_plane))
    through, upstream_sum = prefix((exit_ratio, exit_plane), "gx", compose, identity)
    incoming = through[:, None, None] * inflow + upstream_sum
    return local_part + response[:, :, None, None] * incoming[:, None]


def solution(mesh):
    return jax.shard_map(
        on_device,
        mesh=mesh,
        in_specs=(
            P(None, "gx", "gz", None),
            P("gx", "gz", None),
            P("gx", "gz", None),
            P(None, "gx", None, None),
            P(None, "gx", None),
            P(),
            P(),
            P(),
            P(),
        ),
        out_specs=P(None, "gx", "gz", None),
        check_vma=False,
    )
```

profile of v0, /device:TPU:217, one launch (start us, length us, event | category | flops | bytes accessed | tf_op | source)
XLA Modules:
  0.0 334.0 jit_solution(15417572126514026074)
XLA Ops:
  6.5 1.6 fusion.48
  8.1 1.3 collective-permute-start
  9.4 3.8 %collective-permute-start.1 = (f32[2,2,16,256]{3,2,1,0:T(8,128)}, f32[2,2,16,256]{3,2,1,0:T(8,128)}, u32[]{:S(2)}, u32[]{:S(2)}) collective-permute-start(f32[2,2,16,256]{3,2,1,0:T(8,128)} %get-tuple-element.62), channel_id=1, source_target_pairs={{8,0},{16,8},{24,16},{32,24},{40,32},{48,40},{56,48},{64,56},{72,6... | collective-permute-start | bytes 196616 | tf_op jit(solution)/shard_map/ppermute | solution.py:22
  13.3 3.6 %fusion.47 = (f32[2,128,2,256]{3,2,1,0:T(2,128)}, f32[2,128,2,256]{3,2,1,0:T(2,128)}) fusion(f32[2,128,16,256]{3,2,1,0:T(8,128)} %param.11), kind=kLoop, calls=%fused_computation.82 | loop fusion | bytes 2097152 | tf_op jit(solution)/shard_map/slice | solution.py:20
  16.9 2.9 collective-permute-start.3
  21.1 1.4 slice_bitcast_fusion
  22.5 0.9 slice_reduce_fusion
  23.4 0.8 fusion.44
  24.2 1.3 dynamic-slice
  26.1 0.2 dynamic-update-slice
  26.3 137.6 %all-reduce.2 = (f32[2,16,256]{2,1,0:T(8,128)S(1)}, f32[64]{0:T(128)S(1)}) all-reduce(f32[2,16,256]{2,1,0:T(8,128)S(1)} %fusion.44, f32[64]{0:T(128)S(1)} %dynamic-update-slice), channel_id=1, replica_groups=mesh['gx'=32,'gz'=8] {'gx'}, use_global_device_ids=true, to_apply=%region_0.1 | all-reduce | flops 8256 | bytes 66048 | tf_op jit(solution)/shard_map/psum | solution.py:11
  163.9 22.5 %all_gather.9 = f32[2,128,256]{2,1,0:T(8,128)S(1)} all-gather(f32[2,16,256]{2,1,0:T(8,128)S(1)} %get-tuple-element.53), channel_id=1, replica_groups=mesh['gx'=32,'gz'=8] {'gz'}, dimensions={1}, use_global_device_ids=true | all-gather | bytes 294912 | tf_op jit(solution)/shard_map/all_gather | solution.py:86
  186.4 0.0 copy-start.2
  186.5 6.7 %multiply_bitcast_fusion = (f32[1,128,16,256]{3,2,1,0:T(8,128)S(1)}, f32[128,16,256]{2,1,0:T(8,128)}) fusion(f32[2,128,16,256]{3,2,1,0:T(8,128)} %param.11, f32[128,16,256]{2,1,0:T(8,128)} %param.13), kind=kLoop, calls=%fused_computation.64 | loop fusion | flops 7864320 | bytes 10485760 | tf_op jit(solution)/shard_map/stack | solution.py:62
  193.1 1.6 broadcast_multiply_fusion
  194.7 0.6 multiply_add_fusion.2
  195.4 4.7 %constant_dynamic-update-slice_fusion.1 = f32[2,128,18,256]{3,2,1,0:T(8,128)} fusion(f32[2,128,16,256]{3,2,1,0:T(8,128)} %param.11), kind=kLoop, calls=%fused_computation.78 | loop fusion | bytes 8388608
  200.0 0.9 broadcast_select_fusion.1
  200.9 0.8 broadcast_select_fusion
  201.7 1.1 constant_dynamic-update-slice_fusion
  202.7 25.1 %fusion.8 = f32[2,128,16,256]{3,2,1,0:T(8,128)S(1)} fusion(f32[2,128,16,256]{3,2,1,0:T(8,128)} %param.11, f32[2,2,16,256]{3,2,1,0:T(8,128)S(1)} %broadcast_select_fusion, f32[2,2,16,256]{3,2,1,0:T(8,128)S(1)} %broadcast_select_fusion.1, f32[2,128,2,256]{3,2,1,0:T(2,128)S(1)} %collective-permute-done.2, ...), kind=kLoop, calls=%fused_computation.22 | loop fusion | flops 35651584 | bytes 23724032 | tf_op jit(solution)/shard_map/add | solution.py:63
  227.8 0.0 copy-start.5
  227.8 6.3 %fusion.29 = f32[2,128,16,256]{3,1,2,0:T(8,128)S(1)} fusion(f32[2,128,16,256]{3,2,1,0:T(8,128)S(1)} %fusion.8, f32[2,1,128,128]{3,2,1,0:T(8,128)S(1)} %copy-done), kind=kOutput, calls=%fused_computation.49 | convolution fusion | flops 1610612736 | bytes 8519680 | tf_op jit(solution)/shard_map/sij,sjzy->sizy/dot_general | solution.py:98
  234.2 0.0 copy-start.1
  234.2 2.0 copy-done.1
  236.3 0.6 copy.18
  236.9 0.0 all-gather.4.cloned.1.call-update
  236.9 0.1 reshape.16
  237.0 56.6 %all-gather.4.cloned.1.call-done = f32[64,1,16,256]{3,2,1,0:T(8,128)} async-done(((f32[2,1,16,256]{3,2,1,0:T(8,128)}), f32[64,1,16,256]{3,2,1,0:T(8,128)}) %all-gather.4.cloned.1.call-update) | async-done | bytes 1048592 | tf_op jit(solution)/shard_map/all_gather | solution.py:29
  293.6 26.3 %while.12 = (s32[]{:T(128)}, f32[2]{0:T(128)S(1)}, f32[2,16,256]{2,1,0:T(8,128)S(1)}, s32[]{:T(128)}, f32[32,2]{1,0:T(8,128)S(1)}, /*index=5*/f32[32,2,16,256]{3,2,1,0:T(8,128)}, s32[]{:T(128)}, s32[]{:T(128)}, s32[]{:T(128)}) while((s32[]{:T(128)}, f32[2]{0:T(128)S(1)}, f32[2,16,256]{2,1,0:T(8,128)S(1)}, s32[]{:T(128)}, ...), condition=%wide.region_3.4_spmd, body=%wide.region_2.3_spmd.sunk | while | flops 16391 | bytes 98479 | solution.py:37
  293.6 0.8 bitcast_add_fusion.2
  294.5 0.8 bitcast_add_fusion.2
  295.3 0.8 bitcast_add_fusion.2
  296.2 0.8 bitcast_add_fusion.2
  297.0 0.8 bitcast_add_fusion.2
  297.9 0.8 bitcast_add_fusion.2
  298.7 0.8 bitcast_add_fusion.2
  299.6 0.8 bitcast_add_fusion.2
  300.4 0.8 bitcast_add_fusion.2
  301.3 0.8 bitcast_add_fusion.2
  302.1 0.8 bitcast_add_fusion.2
  302.9 0.8 bitcast_add_fusion.2
  303.8 0.8 bitcast_add_fusion.2
  304.6 0.8 bitcast_add_fusion.2
  305.5 0.8 bitcast_add_fusion.2
  306.3 0.8 bitcast_add_fusion.2
  307.2 0.8 bitcast_add_fusion.2
  308.0 0.8 bitcast_add_fusion.2
  308.9 0.8 bitcast_add_fusion.2
  309.7 0.8 bitcast_add_fusion.2
  310.6 0.8 bitcast_add_fusion.2
  311.4 0.8 bitcast_add_fusion.2
  312.3 0.8 bitcast_add_fusion.2
  313.1 0.8 bitcast_add_fusion.2
  314.0 0.8 bitcast_add_fusion.2
  314.8 0.8 bitcast_add_fusion.2
  315.7 0.8 bitcast_add_fusion.2
  316.5 0.8 bitcast_add_fusion.2
  317.4 0.8 bitcast_add_fusion.2
  318.2 0.8 bitcast_add_fusion.2
  319.1 0.8 bitcast_add_fusion.2
  319.9 0.1 multiply_add_fusion.1
  320.0 2.7 multiply_add_fusion
  322.7 4.4 %copy.19 = f32[2,128,16,256]{3,2,1,0:T(8,128)} copy(f32[2,128,16,256]{3,1,2,0:T(8,128)S(1)} %multiply_add_fusion) | data formatting | bytes 8388608 | tf_op jit(solution)/shard_map/add | solution.py:114
  (51 shorter events, 0.5 us)
Async XLA Ops:
  6.5 221.3 %copy-start = (f32[2,1,128,128]{3,2,1,0:T(8,128)S(1)}, f32[2,1,128,128]{3,2,1,0:T(8,128)}, u32[]{:S(2)}) copy-start(f32[2,1,128,128]{3,2,1,0:T(8,128)} %param.14) | copy-start | bytes 393220
  6.5 287.1 %all-gather.4.cloned.1.call-start = ((), (), s32[]{:S(2)}) async-start(), calls=%async_computation | async-start | bytes 1081344 | tf_op jit(solution)/shard_map/all_gather | solution.py:29
  8.1 191.9 %collective-permute-start = (f32[2,2,16,256]{3,2,1,0:T(8,128)}, f32[2,2,16,256]{3,2,1,0:T(8,128)}, u32[]{:S(2)}, u32[]{:S(2)}) collective-permute-start(f32[2,2,16,256]{3,2,1,0:T(8,128)} %get-tuple-element.61), channel_id=1, source_target_pairs={{0,8},{8,16},{16,24},{24,32},{32,40},{40,48},{48,56},{56,64},{64,7... | collective-permute-start | bytes 196616 | tf_op jit(solution)/shard_map/ppermute | solution.py:21
  9.4 191.5 %collective-permute-start.1 = (f32[2,2,16,256]{3,2,1,0:T(8,128)}, f32[2,2,16,256]{3,2,1,0:T(8,128)}, u32[]{:S(2)}, u32[]{:S(2)}) collective-permute-start(f32[2,2,16,256]{3,2,1,0:T(8,128)} %get-tuple-element.62), channel_id=1, source_target_pairs={{8,0},{16,8},{24,16},{32,24},{40,32},{48,40},{56,48},{64,56},{72,6... | collective-permute-start | bytes 196616 | tf_op jit(solution)/shard_map/ppermute | solution.py:22
  16.9 184.8 %collective-permute-start.3 = (f32[2,128,2,256]{3,2,1,0:T(2,128)}, f32[2,128,2,256]{3,2,1,0:T(2,128)S(1)}, u32[]{:S(2)}, u32[]{:S(2)}) collective-permute-start(f32[2,128,2,256]{3,2,1,0:T(2,128)} %get-tuple-element.59), channel_id=1, source_target_pairs={{1,0},{2,1},{3,2},{4,3},{5,4},{6,5},{7,6},{0,7},{9,8},{10,9},{11,1... | collective-permute-start | bytes 1572872 | tf_op jit(solution)/shard_map/ppermute | solution.py:22
  19.8 182.9 %collective-permute-start.2 = (f32[2,128,2,256]{3,2,1,0:T(2,128)}, f32[2,128,2,256]{3,2,1,0:T(2,128)S(1)}, u32[]{:S(2)}, u32[]{:S(2)}) collective-permute-start(f32[2,128,2,256]{3,2,1,0:T(2,128)} %get-tuple-element.60), channel_id=1, source_target_pairs={{0,1},{1,2},{2,3},{3,4},{4,5},{5,6},{6,7},{7,0},{8,9},{9,10},{10,1... | collective-permute-start | bytes 1572872 | tf_op jit(solution)/shard_map/ppermute | solution.py:21
  186.4 6.7 %copy-start.2 = (f32[128,16,256]{2,1,0:T(8,128)S(1)}, f32[128,16,256]{2,1,0:T(8,128)}, u32[]{:S(2)}) copy-start(f32[128,16,256]{2,1,0:T(8,128)} %param.12) | copy-start | bytes 6291460
  193.1 1.6 copy-start.3
  193.1 1.6 copy-start.4
  227.8 92.1 %copy-start.5 = (f32[2,1,128]{2,1,0:T(1,128)S(1)}, f32[2,1,128]{2,1,0:T(1,128)}, u32[]{:S(2)}) copy-start(f32[2,1,128]{2,1,0:T(1,128)} %param.15) | copy-start | bytes 3076
  234.2 2.0 copy-start.1
Sparse Core Ops, SparseCore 0:
  237.0 56.5 all-gather.3
where the time goes:
time: 337 us; the launch traced here: 334 us
  blocking collectives  160 us (47%)
  other arithmetic  65.5 us (19%)
  waiting for transfers between devices  56.6 us (17%)
  local copies, waits for them, and re-layouts  21.9 us (6%)
  between operations  15.5 us (5%)
  starting transfers between devices  8.06 us (2%)
  matrix products  6.35 us (2%)
    psum x1, blocking collectives, from_root(): return lax.psum(jnp.where(mine, x, jnp.zeros_like(x)), axis)  138 us
    all_gather x1, waiting for transfers between devices, prefix(): gathered = jax.tree.map(lambda a: lax.all_gather(a, axis), part)  56.6 us
    add x31, other arithmetic, compose(): later_part[0][:, None, None] * earlier_part[1] + later_part[1]  25.9 us
    add x1, other arithmetic, explicit_part(): return center + diffusivity[None] * laplacian + source  25.1 us
    all_gather x1, blocking collectives, on_device(): station_plane = lax.all_gather(arrived, 'gz', axis=1, tiled=True)  22.5 us
    unnamed x16, local copies, waits for them, and re-layouts  8.19 us
    ppermute x2, starting transfers between devices, with_halo(): after = lax.ppermute(first, axis, down)  6.77 us
  transfers between devices with their start and end apart: 5, of which 1 were waited for; matrix products, arithmetic and copies ran while one was open for 7% of the time, Pallas kernels for 0%

commit v1 on v0

--- a/solution.py
+++ b/solution.py
@@ -83,7 +83,9 @@
     local_plane = station_index[0] - owner_row * plane_count
     own_slice = lax.dynamic_index_in_dim(scalars, local_plane, 1, keepdims=False)
     arrived = from_root(own_slice, "gx", owner_row)
-    station_plane = lax.all_gather(arrived, "gz", axis=1, tiled=True)
+    station_plane = jnp.concatenate(
+        lax.all_to_all(jnp.stack([arrived] * lax.axis_size("gz")), "gz", 0, 0), axis=1
+    )
     inflow_full = make_inflow(station_plane, mean_profile, recycle_gain, span_shift)
     inflow = lax.dynamic_slice_in_dim(inflow_full, span_rank * span_cells, span_cells, 1)
     stream_padded = with_halo(scalars, (("gx", 1),), 2, False)

time: 337 us -> 309 us (0.917)
  blocking collectives: 160 us -> 138 us
  waiting for transfers between devices: 56.6 us -> 50.1 us
  starting transfers between devices: 8.06 us -> 12.4 us
    all_gather x1 -> x0, blocking collectives: 22.5 us -> none  [on_device(): station_plane = lax.all_gather(arrived, 'gz', axis=1, tiled=True)]
    all_gather x1, waiting for transfers between devices: 56.6 us -> 49.6 us  [prefix(): gathered = jax.tree.map(lambda a: lax.all_gather(a, axis), part)]
    all_to_all x0 -> x1, starting transfers between devices: none -> 4.48 us  [on_device(): lax.all_to_all(jnp.stack([arrived] * lax.axis_size('gz')), 'gz', 0, 0)]
    unnamed x16 -> x18, local copies, waits for them, and re-layouts: 8.19 us -> 7.36 us
  transfers between devices with their start and end apart: 5 -> 6, of which waited for: 1 -> 2; matrix products, arithmetic and copies ran while one was open for 7% -> 6% of each run, Pallas kernels for 0% -> 0%
where the time goes in v1:
time: 309 us; the launch traced here: 306 us
  blocking collectives  138 us (45%)
  other arithmetic  63.2 us (20%)
  waiting for transfers between devices  50.1 us (16%)
  local copies, waits for them, and re-layouts  20.7 us (7%)
  between operations  15.6 us (5%)
  starting transfers between devices  12.4 us (4%)
  matrix products  6.35 us (2%)
    psum x1, blocking collectives, from_root(): return lax.psum(jnp.where(mine, x, jnp.zeros_like(x)), axis)  138 us
    all_gather x1, waiting for transfers between devices, prefix(): gathered = jax.tree.map(lambda a: lax.all_gather(a, axis), part)  49.6 us
    add x31, other arithmetic, compose(): later_part[0][:, None, None] * earlier_part[1] + later_part[1]  25.9 us
    add x1, other arithmetic, explicit_part(): return center + diffusivity[None] * laplacian + source  25 us
    unnamed x18, local copies, waits for them, and re-layouts  7.36 us
    another operation x1, other arithmetic, explicit_part(): jnp.stack([reaction_yields[0] * reaction, reaction_yields[1] * reaction])  6.69 us
    ppermute x2, starting transfers between devices, with_halo(): after = lax.ppermute(first, axis, down)  6.56 us
    dot_general x1, matrix products, on_device(): jnp.einsum('sij,sjzy->sizy', block_inverse[:, 0], explicit, precision=lax...  6.35 us
  transfers between devices with their start and end apart: 6, of which 2 were waited for; matrix products, arithmetic and copies ran while one was open for 6% of the time, Pallas kernels for 0%

profile of v1, /device:TPU:217, one launch (start us, length us, event | category | flops | bytes accessed | tf_op | source)
XLA Modules:
  0.0 306.2 jit_solution(1782909083492430511)
XLA Ops:
  7.3 0.9 slice_reduce_fusion
  8.1 1.3 dynamic-slice
  10.0 0.8 select_bitcast_fusion
  10.8 0.2 dynamic-update-slice
  11.1 137.7 %all-reduce.2 = (f32[2,16,256]{2,1,0:T(8,128)S(1)}, f32[64]{0:T(128)S(1)}) all-reduce(f32[2,16,256]{2,1,0:T(8,128)S(1)} %get-tuple-element.61, f32[64]{0:T(128)S(1)} %dynamic-update-slice), channel_id=1, replica_groups=mesh['gx'=32,'gz'=8] {'gx'}, use_global_device_ids=true, to_apply=%region_0.1 | all-reduce | flops 8256 | bytes 66048 | tf_op jit(solution)/shard_map/psum | solution.py:11
  148.8 0.7 stack.8
  149.5 4.5 %all-to-all-start = ((f32[8,2,16,256]{3,2,1,0:T(8,128)}), f32[8,2,16,256]{3,2,1,0:T(8,128)S(1)}, u32[]{:S(2)}, u32[]{:S(2)}) async-start(f32[8,2,16,256]{3,2,1,0:T(8,128)} %stack.8), calls=%async_computation | async-start | bytes 524288 | tf_op jit(solution)/shard_map/all_to_all | solution.py:87
  154.0 0.0 all-gather.4.cloned.1.call-start
  154.0 0.9 fusion.47
  154.9 1.3 collective-permute-start
  156.2 3.0 collective-permute-start.1
  159.3 3.6 %fusion.46 = (f32[2,128,2,256]{3,2,1,0:T(2,128)}, f32[2,128,2,256]{3,2,1,0:T(2,128)}) fusion(f32[2,128,16,256]{3,2,1,0:T(8,128)} %param.11), kind=kLoop, calls=%fused_computation.82 | loop fusion | bytes 2097152 | tf_op jit(solution)/shard_map/slice | solution.py:20
  162.9 3.5 %collective-permute-start.3 = (f32[2,128,2,256]{3,2,1,0:T(2,128)}, f32[2,128,2,256]{3,2,1,0:T(2,128)}, u32[]{:S(2)}, u32[]{:S(2)}) collective-permute-start(f32[2,128,2,256]{3,2,1,0:T(2,128)} %get-tuple-element.59), channel_id=1, source_target_pairs={{1,0},{2,1},{3,2},{4,3},{5,4},{6,5},{7,6},{0,7},{9,8},{10,9},{11,1... | collective-permute-start | bytes 1572872 | tf_op jit(solution)/shard_map/ppermute | solution.py:22
  166.4 0.0 collective-permute-start.2
  166.4 6.7 %multiply_bitcast_fusion = (f32[1,128,16,256]{3,2,1,0:T(8,128)S(1)}, f32[128,16,256]{2,1,0:T(8,128)}) fusion(f32[2,128,16,256]{3,2,1,0:T(8,128)} %param.11, f32[128,16,256]{2,1,0:T(8,128)} %param.13), kind=kLoop, calls=%fused_computation.64 | loop fusion | flops 7864320 | bytes 10485760 | tf_op jit(solution)/shard_map/stack | solution.py:62
  173.1 1.6 broadcast_multiply_fusion
  174.7 1.4 copy-done.1
  176.1 2.5 constant_dynamic-update-slice_fusion.1
  179.4 2.1 constant_dynamic-update-slice_fusion
  181.5 0.5 collective-permute-done.2
  182.0 25.0 %fusion.8 = f32[2,128,16,256]{3,2,1,0:T(8,128)S(1)} fusion(f32[2,128,16,256]{3,2,1,0:T(8,128)} %param.11, f32[2,2,16,256]{3,2,1,0:T(8,128)S(1)} %broadcast_select_fusion, f32[2,2,16,256]{3,2,1,0:T(8,128)S(1)} %broadcast_select_fusion.1, f32[2,128,2,256]{3,2,1,0:T(2,128)S(1)} %collective-permute-done.2, ...), kind=kLoop, calls=%fused_computation.22 | loop fusion | flops 35651584 | bytes 23724032 | tf_op jit(solution)/shard_map/add | solution.py:63
  207.0 0.0 copy-start.6
  207.0 6.3 %fusion.29 = f32[2,128,16,256]{3,1,2,0:T(8,128)S(1)} fusion(f32[2,128,16,256]{3,2,1,0:T(8,128)S(1)} %fusion.8, f32[2,1,128,128]{3,2,1,0:T(8,128)S(1)} %copy-done), kind=kOutput, calls=%fused_computation.49 | convolution fusion | flops 1610612736 | bytes 8519680 | tf_op jit(solution)/shard_map/sij,sjzy->sizy/dot_general | solution.py:100
  213.4 0.0 copy-start.2
  213.4 2.0 copy-done.2
  215.4 0.6 copy.19
  216.0 0.0 all-gather.4.cloned.1.call-update
  216.0 0.1 reshape.26
  216.1 49.6 %all-gather.4.cloned.1.call-done = f32[64,1,16,256]{3,2,1,0:T(8,128)} async-done(((f32[2,1,16,256]{3,2,1,0:T(8,128)}), f32[64,1,16,256]{3,2,1,0:T(8,128)}) %all-gather.4.cloned.1.call-update) | async-done | bytes 1048592 | tf_op jit(solution)/shard_map/all_gather | solution.py:29
  265.8 26.3 %while.12 = (s32[]{:T(128)}, f32[2]{0:T(128)S(1)}, f32[2,16,256]{2,1,0:T(8,128)S(1)}, s32[]{:T(128)}, f32[32,2]{1,0:T(8,128)S(1)}, /*index=5*/f32[32,2,16,256]{3,2,1,0:T(8,128)}, s32[]{:T(128)}, s32[]{:T(128)}, s32[]{:T(128)}) while((s32[]{:T(128)}, f32[2]{0:T(128)S(1)}, f32[2,16,256]{2,1,0:T(8,128)S(1)}, s32[]{:T(128)}, ...), condition=%wide.region_3.4_spmd, body=%wide.region_2.3_spmd.sunk | while | flops 16391 | bytes 98479 | solution.py:37
  265.8 0.8 bitcast_add_fusion.2
  266.6 0.8 bitcast_add_fusion.2
  267.5 0.8 bitcast_add_fusion.2
  268.3 0.8 bitcast_add_fusion.2
  269.2 0.8 bitcast_add_fusion.2
  270.0 0.8 bitcast_add_fusion.2
  270.9 0.8 bitcast_add_fusion.2
  271.7 0.8 bitcast_add_fusion.2
  272.6 0.8 bitcast_add_fusion.2
  273.4 0.8 bitcast_add_fusion.2
  274.3 0.8 bitcast_add_fusion.2
  275.1 0.8 bitcast_add_fusion.2
  276.0 0.8 bitcast_add_fusion.2
  276.8 0.8 bitcast_add_fusion.2
  277.7 0.8 bitcast_add_fusion.2
  278.5 0.8 bitcast_add_fusion.2
  279.4 0.8 bitcast_add_fusion.2
  280.2 0.8 bitcast_add_fusion.2
  281.0 0.8 bitcast_add_fusion.2
  281.9 0.8 bitcast_add_fusion.2
  282.7 0.8 bitcast_add_fusion.2
  283.6 0.8 bitcast_add_fusion.2
  284.4 0.8 bitcast_add_fusion.2
  285.3 0.8 bitcast_add_fusion.2
  286.1 0.8 bitcast_add_fusion.2
  287.0 0.8 bitcast_add_fusion.2
  287.8 0.8 bitcast_add_fusion.2
  288.7 0.8 bitcast_add_fusion.2
  289.5 0.8 bitcast_add_fusion.2
  290.4 0.8 bitcast_add_fusion.2
  291.2 0.8 bitcast_add_fusion.2
  292.1 0.1 multiply_add_fusion.1
  292.1 2.7 multiply_add_fusion
  294.9 4.4 %copy.20 = f32[2,128,16,256]{3,2,1,0:T(8,128)} copy(f32[2,128,16,256]{3,1,2,0:T(8,128)S(1)} %multiply_add_fusion) | data formatting | bytes 8388608 | tf_op jit(solution)/shard_map/add | solution.py:116
  (55 shorter events, 0.6 us)
Async XLA Ops:
  6.5 200.4 %copy-start = (f32[2,1,128,128]{3,2,1,0:T(8,128)S(1)}, f32[2,1,128,128]{3,2,1,0:T(8,128)}, u32[]{:S(2)}) copy-start(f32[2,1,128,128]{3,2,1,0:T(8,128)} %param.14) | copy-start | bytes 393220
  149.5 29.7 %all-to-all-start = ((f32[8,2,16,256]{3,2,1,0:T(8,128)}), f32[8,2,16,256]{3,2,1,0:T(8,128)S(1)}, u32[]{:S(2)}, u32[]{:S(2)}) async-start(f32[8,2,16,256]{3,2,1,0:T(8,128)} %stack.8), calls=%async_computation | async-start | bytes 524288 | tf_op jit(solution)/shard_map/all_to_all | solution.py:87
  154.0 111.8 %all-gather.4.cloned.1.call-start = ((), (), s32[]{:S(2)}) async-start(), calls=%async_computation.1 | async-start | bytes 1081344 | tf_op jit(solution)/shard_map/all_gather | solution.py:29
  154.9 24.5 %collective-permute-start = (f32[2,2,16,256]{3,2,1,0:T(8,128)S(1)}, f32[2,2,16,256]{3,2,1,0:T(8,128)S(1)}, u32[]{:S(2)}, u32[]{:S(2)}) collective-permute-start(f32[2,2,16,256]{3,2,1,0:T(8,128)S(1)} %get-tuple-element.63), channel_id=1, source_target_pairs={{0,8},{8,16},{16,24},{24,32},{32,40},{40,48},{48,56},{56,64},{64,7... | collective-permute-start | bytes 196616 | tf_op jit(solution)/shard_map/ppermute | solution.py:21
  156.2 23.0 %collective-permute-start.1 = (f32[2,2,16,256]{3,2,1,0:T(8,128)S(1)}, f32[2,2,16,256]{3,2,1,0:T(8,128)S(1)}, u32[]{:S(2)}, u32[]{:S(2)}) collective-permute-start(f32[2,2,16,256]{3,2,1,0:T(8,128)S(1)} %get-tuple-element.64), channel_id=1, source_target_pairs={{8,0},{16,8},{24,16},{32,24},{40,32},{48,40},{56,48},{64,56},{72,6... | collective-permute-start | bytes 196616 | tf_op jit(solution)/shard_map/ppermute | solution.py:22
  162.9 16.5 %collective-permute-start.3 = (f32[2,128,2,256]{3,2,1,0:T(2,128)}, f32[2,128,2,256]{3,2,1,0:T(2,128)}, u32[]{:S(2)}, u32[]{:S(2)}) collective-permute-start(f32[2,128,2,256]{3,2,1,0:T(2,128)} %get-tuple-element.59), channel_id=1, source_target_pairs={{1,0},{2,1},{3,2},{4,3},{5,4},{6,5},{7,6},{0,7},{9,8},{10,9},{11,1... | collective-permute-start | bytes 1572872 | tf_op jit(solution)/shard_map/ppermute | solution.py:22
  166.4 6.7 %copy-start.3 = (f32[128,16,256]{2,1,0:T(8,128)S(1)}, f32[128,16,256]{2,1,0:T(8,128)}, u32[]{:S(2)}) copy-start(f32[128,16,256]{2,1,0:T(8,128)} %param.12) | copy-start | bytes 6291460
  166.4 15.5 %collective-permute-start.2 = (f32[2,128,2,256]{3,2,1,0:T(2,128)}, f32[2,128,2,256]{3,2,1,0:T(2,128)S(1)}, u32[]{:S(2)}, u32[]{:S(2)}) collective-permute-start(f32[2,128,2,256]{3,2,1,0:T(2,128)} %get-tuple-element.60), channel_id=1, source_target_pairs={{0,1},{1,2},{2,3},{3,4},{4,5},{5,6},{6,7},{7,0},{8,9},{9,10},{10,1... | collective-permute-start | bytes 1572872 | tf_op jit(solution)/shard_map/ppermute | solution.py:21
  173.1 2.9 copy-start.1
  176.1 3.3 %copy-start.4 = (f32[2,256]{1,0:T(2,128)S(1)}, f32[2,256]{1,0:T(2,128)}, u32[]{:S(2)}) copy-start(f32[2,256]{1,0:T(2,128)} %param.16) | copy-start | bytes 6148
  176.1 3.3 %copy-start.5 = (f32[2,256]{1,0:T(2,128)S(1)}, f32[2,256]{1,0:T(2,128)}, u32[]{:S(2)}) copy-start(f32[2,256]{1,0:T(2,128)} %param.17) | copy-start | bytes 6148
  207.0 85.1 %copy-start.6 = (f32[2,1,128]{2,1,0:T(1,128)S(1)}, f32[2,1,128]{2,1,0:T(1,128)}, u32[]{:S(2)}) copy-start(f32[2,1,128]{2,1,0:T(1,128)} %param.15) | copy-start | bytes 3076
  213.4 2.0 copy-start.2
Sparse Core Ops, SparseCore 0:
  216.2 49.5 all-gather.3
